TPU v7x, 512 devices: a whole 4x4x16 slice. The times are simulated.
512 devices in a mesh: ctx: 64 (over x_hi, z, core), mp: 8 (over x_lo, y).
Axes of the slice: x: 4 (x_hi: 2, x_lo: 2; x = x_hi * 2 + x_lo), y: 4, z: 16, core: 2. Of those that a mesh axis runs over, the one named last changes fastest.
Arguments:
- queries: bfloat16 [4096, 8192], P('ctx', 'mp'), may hold values from -8 to 8
- keys: bfloat16 [4096, 1024], P('ctx', 'mp'), may hold values from -8 to 8
- values: bfloat16 [4096, 1024], P('ctx', 'mp'), may hold values from -6 to 6
- positions: int32 [4096], P('ctx'), may hold values from 0 to 4095, as said below
- x_normed: bfloat16 [4096, 8192], P('ctx', 'mp'), may hold values from -6 to 6
- w_gate: bfloat16 [8192, 16384], P('mp', 'ctx'), may hold values from -0.0625 to 0.0625
- w_up: bfloat16 [8192, 16384], P('mp', 'ctx'), may hold values from -0.0625 to 0.0625
Outputs:
- attended: bfloat16 [4096, 8192], P('ctx', 'mp')
- mlp_hidden: bfloat16 [4096, 16384], P('mp', 'ctx')
Inputs may be any that keep to these rules, and one draw needn't show every extreme that they name: `positions`: each position of 0 to 4095 appears exactly once.
All inputs are finite; a program needn't handle non-finite values.
Results may differ from a plain program's by a relative error of at most 0.02.
Values may be sent and summed in bfloat16 or wider, within the bound.
No kernel may reach another device: no remote copies, remote signals or barrier semaphores. Data moves between devices by JAX's collectives and lax.ppermute only.
A program may use at most 64 MiB of HBM per device.

v0:
```python
import jax
import jax.numpy as jnp
from jax import lax
from jax.sharding import Mesh, PartitionSpec as P

HEAD = 128
CTX = ("xh", "zz", "cc")


def per_device(queries, keys, values, positions, x_normed, w_gate, w_up):
    tok_rows = queries.shape[0]
    local_heads = queries.shape[1] // HEAD
    local_kv = keys.shape[1] // HEAD
    group = local_heads // local_kv
    scale = HEAD ** (-0.5)
    query_four = queries.reshape(tok_rows, local_kv, group, HEAD)
    top_run = jnp.full((local_kv, group, tok_rows), -1e30, jnp.float32)
    pos_hi = positions // 64
    pos_lo = positions - pos_hi * 64
    pos_cols = jnp.zeros((tok_rows, HEAD), jnp.bfloat16)
    pos_cols = pos_cols.at[:, 0].set(pos_hi.astype(jnp.bfloat16))
    pos_cols = pos_cols.at[:, 1].set(pos_lo.astype(jnp.bfloat16))
    kv_pack = jnp.concatenate((keys, values, pos_cols), axis=1)
    kv_all = lax.all_gather(kv_pack, CTX, axis=0, tiled=True)
    kv_width = keys.shape[1]
    k_piece = kv_all[:, :kv_width]
    v_piece = kv_all[:, kv_width : 2 * kv_width]
    pos_back = kv_all[:, 2 * kv_width :].astype(jnp.float32)
    k_pos = pos_back[:, 0] * 64.0 + pos_back[:, 1]
    q_pos = positions.astype(jnp.float32)
    count = k_piece.shape[0]
    k_three = k_piece.reshape(count, local_kv, HEAD)
    v_three = v_piece.reshape(count, local_kv, HEAD)
    scores = (
        jnp.einsum("tgjd,sgd->gjts", query_four, k_three, preferred_element_type=jnp.float32)
        * scale
    )
    visible = k_pos[None, :] <= q_pos[:, None]
    piece_top = jnp.max(jnp.where(visible, scores, jnp.float32(-1e30)), axis=-1)
    top_new = jnp.maximum(top_run, piece_top)
    weights = jnp.where(visible, jnp.exp(scores - top_new[..., None]), jnp.float32(0.0))
    total_new = jnp.sum(weights, axis=-1)
    mixed = jnp.einsum(
        "gjts,sgd->gjtd", weights.astype(jnp.bfloat16), v_three, preferred_element_type=jnp.float32
    )
    final_state = (top_new, total_new, mixed)
    top_run, total_run, accum = final_state
    normed = accum / total_run[..., None]
    attended = (
        jnp.transpose(normed, (2, 0, 1, 3))
        .reshape(tok_rows, local_heads * HEAD)
        .astype(jnp.bfloat16)
    )
    hidden_cols = w_gate.shape[1]
    both_weights = jnp.concatenate((w_gate, w_up), axis=1)
    pair_weights = lax.all_gather(both_weights, "cc", axis=1, tiled=True)
    x_half = lax.all_gather(x_normed, ("xh", "zz"), axis=0, tiled=True)
    block_terms = jnp.dot(x_half, pair_weights, preferred_element_type=jnp.float32).astype(
        jnp.bfloat16
    )
    summed = lax.psum_scatter(block_terms, "mp", scatter_dimension=0, tiled=True).astype(
        jnp.float32
    )
    width = 2 * hidden_cols
    per_core = []
    for owner in range(2):
        gate = summed[:, owner * width : owner * width + hidden_cols]
        up = summed[:, owner * width + hidden_cols : (owner + 1) * width]
        per_core.append((jax.nn.silu(gate) * up).astype(jnp.bfloat16))
    stacked = jnp.stack(per_core)
    core = lax.axis_index("cc")
    mine = stacked[core]
    other = stacked[1 - core]
    got = lax.ppermute(other, "cc", [(0, 1), (1, 0)])
    both = jnp.stack((mine, got))
    parity0 = both[core]
    parity1 = both[1 - core]
    rows = parity0.shape[0]
    chunk = tok_rows
    mlp_hidden = jnp.stack(
        (
            parity0.reshape(rows // chunk, chunk, hidden_cols),
            parity1.reshape(rows // chunk, chunk, hidden_cols),
        ),
        axis=1,
    ).reshape(2 * rows, hidden_cols)
    return (attended, mlp_hidden)


def solution(mesh):
    n_ctx = mesh.shape["ctx"]
    n_mp = mesh.shape["mp"]
    fine = Mesh(mesh.devices.reshape(2, n_ctx // 4, 2, n_mp), ("xh", "zz", "cc", "mp"))
    return jax.shard_map(
        per_device,
        mesh=fine,
        in_specs=(
            P(CTX, "mp"),
            P(CTX, "mp"),
            P(CTX, "mp"),
            P(CTX),
            P(CTX, "mp"),
            P("mp", CTX),
            P("mp", CTX),
        ),
        out_specs=(P(CTX, "mp"), P("mp", CTX)),
        check_vma=False,
    )
```

profile of v0, /device:TPU:1, one launch (start us, length us, event | category | flops | bytes accessed | tf_op | source)
XLA Modules:
  0.0 425.7 jit_solution(6835526162539869750)
XLA Ops:
  7.2 0.0 copy-start
  7.2 0.0 all-gather.6.cloned.1.call-start
  7.2 2.3 pad_maximum_fusion
  9.5 0.0 all-gather.6.cloned.1.call-update
  9.5 0.0 all-gather.8.cloned.1.call-start
  9.6 0.7 all-gather.8.cloned.1.call-update
  10.3 0.0 all-gather.4.cloned.1.call-start
  10.3 0.6 compare_reduce_fusion.1
  11.0 0.6 compare_reduce_fusion
  11.6 1.3 fusion.32
  12.9 0.7 fusion.31
  13.6 0.1 copy.18
  13.7 0.1 copy.19
  13.8 0.1 scatter.9
  14.0 1.4 pad_maximum_fusion.2
  15.3 0.0 all-gather.4.cloned.1.call-update
  15.4 0.0 reduce-scatter.2.cloned.1.call-start
  15.4 22.5 %all-gather.6.cloned.1.call-done = bf16[1024,1024]{1,0:T(8,128)(2,1)} async-done(((bf16[1024,512]{1,0:T(8,128)(2,1)}), bf16[1024,1024]{1,0:T(8,128)(2,1)}) %all-gather.6.cloned.1.call-update) | async-done | bytes 2097168 | tf_op jit(solution)/shard_map/all_gather | solution.py:56
  37.9 157.3 %all-gather.8.cloned.1.call-done = bf16[2048,1024]{1,0:T(8,128)(2,1)} async-done(((bf16[64,1024]{1,0:T(8,128)(2,1)}), bf16[2048,1024]{1,0:T(8,128)(2,1)}) %all-gather.8.cloned.1.call-update) | async-done | bytes 4194320 | tf_op jit(solution)/shard_map/all_gather | solution.py:57
  195.2 9.3 %convert_bitcast_fusion = bf16[2048,1024]{0,1:T(8,128)(2,1)} fusion(bf16[1024,1024]{1,0:T(8,128)(2,1)} %all-gather.6.cloned.1.call-done, bf16[2048,1024]{1,0:T(8,128)(2,1)} %all-gather.8.cloned.1.call-done), kind=kOutput, calls=%fused_computation.8 | convolution fusion | flops 4297064448 | bytes 10485760 | tf_op jit(solution)/shard_map/dot_general | solution.py:58
  204.5 0.0 copy-start.3
  204.5 0.0 reduce-scatter.2.cloned.1.call-update
  204.5 0.6 copy-done.3
  205.2 145.6 %all-gather.4.cloned.1.call-done = bf16[4096,384]{1,0:T(8,128)(2,1)} async-done(((bf16[64,384]{1,0:T(8,128)(2,1)}), bf16[4096,384]{1,0:T(8,128)(2,1)}) %all-gather.4.cloned.1.call-update) | async-done | bytes 3145744 | tf_op jit(solution)/shard_map/all_gather | solution.py:24
  350.8 0.0 copy-start.2
  350.8 1.5 slice_convert_fusion
  352.3 1.2 fusion.9
  353.5 0.2 broadcast_compare_fusion
  353.7 0.0 copy-done
  353.7 0.0 copy-done.2
  353.7 1.7 fusion
  355.4 0.0 copy-start.1
  355.4 3.2 copy-done.1
  358.6 2.4 fusion.3
  361.0 47.3 %reduce-scatter.2.cloned.1.call-done = bf16[256,1024]{0,1:T(8,128)(2,1)} async-done(((bf16[2048,1024]{0,1:T(8,128)(2,1)}), bf16[256,1024]{0,1:T(8,128)(2,1)}) %reduce-scatter.2.cloned.1.call-update) | async-done | bytes 524304 | tf_op jit(solution)/shard_map/reduce_scatter | solution.py:61
  408.3 1.1 convert_element_type.53
  409.4 0.2 fusion.30
  409.6 0.1 fusion.25
  409.7 2.6 collective-permute-start
  412.4 4.9 %fusion.16 = bf16[64,1,8,128]{3,0,2,1:T(8,128)(2,1)S(1)} fusion(f32[4096,64,8]{0,1,2:T(8,128)} %copy-done.1, f32[8,64]{1,0:T(8,128)S(1)} %broadcast_maximum_fusion, pred[64,4096]{1,0:T(8,128)(4,1)S(1)} %broadcast_compare_fusion, bf16[4096,384]{1,0:T(8,128)(2,1)S(1)} %copy-done.2, f32[8,64]{1,0:T(8,128)S(1)} %fusion.3), kind=kOutput, calls=%fused_computation.16 | convolution fusion | flops 545390592 | bytes 9838592 | tf_op jit(solution)/shard_map/gjts,sgd->gjtd/dot_general | solution.py:43
  417.3 0.1 copy.21
  417.4 0.7 copy.34
  418.1 0.0 collective-permute-done
  418.1 0.1 fusion.23
  418.2 0.1 copy.23
  418.3 0.1 copy.22
  418.4 0.7 copy.24
  (4 shorter events, 0.0 us)
Async XLA Ops:
  7.2 346.5 %copy-start = (bf16[64,1024]{1,0:T(8,128)(2,1)S(1)}, bf16[64,1024]{1,0:T(8,128)(2,1)}, u32[]{:S(2)}) copy-start(bf16[64,1024]{1,0:T(8,128)(2,1)} %param.11) | copy-start | bytes 393220
  7.2 30.7 %all-gather.6.cloned.1.call-start = ((), (), s32[]{:S(2)}) async-start(), calls=%async_computation.2 | async-start | bytes 3145728 | tf_op jit(solution)/shard_map/all_gather | solution.py:56
  9.5 185.7 %all-gather.8.cloned.1.call-start = ((), (), s32[]{:S(2)}) async-start(), calls=%async_computation.3 | async-start | bytes 4325376 | tf_op jit(solution)/shard_map/all_gather | solution.py:57
  10.3 340.5 %all-gather.4.cloned.1.call-start = ((), (), s32[]{:S(2)}) async-start(), calls=%async_computation.1 | async-start | bytes 3194880 | tf_op jit(solution)/shard_map/all_gather | solution.py:24
  15.4 392.9 %reduce-scatter.2.cloned.1.call-start = ((), (), s32[]{:S(2)}) async-start(), calls=%async_computation.4 | async-start | bytes 4718592 | tf_op jit(solution)/shard_map/reduce_scatter | solution.py:61
  204.5 0.7 copy-start.3
  350.8 2.9 copy-start.2
  355.4 3.2 copy-start.1
  409.7 8.3 %collective-permute-start = (bf16[256,256]{0,1:T(8,128)(2,1)S(1)}, bf16[256,256]{0,1:T(8,128)(2,1)S(1)}, u32[]{:S(2)}, u32[]{:S(2)}) collective-permute-start(bf16[256,256]{0,1:T(8,128)(2,1)S(1)} %get-tuple-element.32), channel_id=1, source_target_pairs={{0,8},{8,0},{1,9},{9,1},{2,10},{10,2},{3,11},{11,3},{4,12},{12,4},... | collective-permute-start | bytes 393224 | tf_op jit(solution)/shard_map/ppermute | solution.py:74
Sparse Core Ops, SparseCore 0:
  10.1 27.7 all-gather.5
  41.0 154.1 all-gather.7
  199.1 151.6 all-gather.3
  353.5 54.7 reduce-scatter.1
where the time goes:
time: 426 us
  waiting for transfers between devices  373 us (88%)
  matrix products  15.9 us (4%)
  between operations  13.9 us (3%)
  other arithmetic  13.8 us (3%)
  local copies, waits for them, and re-layouts  5.9 us (1%)
    all_gather x1, waiting for transfers between devices, per_device(): x_half = lax.all_gather(x_normed, ('xh', 'zz'), axis=0, tiled=True)  157 us
    all_gather x1, waiting for transfers between devices, per_device(): kv_all = lax.all_gather(kv_pack, CTX, axis=0, tiled=True)  146 us
    reduce_scatter x1, waiting for transfers between devices, per_device(): lax.psum_scatter(block_terms, 'mp', scatter_dimension=0, tiled=True)  47.3 us
    all_gather x1, waiting for transfers between devices, per_device(): pair_weights = lax.all_gather(both_weights, 'cc', axis=1, tiled=True)  22.5 us
    dot_general x1, matrix products, per_device(): jnp.dot(x_half, pair_weights, preferred_element_type=jnp.float32)  9.31 us
  transfers between devices with their start and end apart: 5, of which 4 were waited for; matrix products, arithmetic and copies ran while one was open for 6% of the time, Pallas kernels for 0%

commit v1 on v0

--- a/solution.py
+++ b/solution.py
@@ -21,7 +21,9 @@
     pos_cols = pos_cols.at[:, 0].set(pos_hi.astype(jnp.bfloat16))
     pos_cols = pos_cols.at[:, 1].set(pos_lo.astype(jnp.bfloat16))
     kv_pack = jnp.concatenate((keys, values, pos_cols), axis=1)
-    kv_all = lax.all_gather(kv_pack, CTX, axis=0, tiled=True)
+    kv_all = jnp.concatenate(
+        lax.all_to_all(jnp.stack([kv_pack] * lax.axis_size(CTX)), CTX, 0, 0), axis=0
+    )
     kv_width = keys.shape[1]
     k_piece = kv_all[:, :kv_width]
     v_piece = kv_all[:, kv_width : 2 * kv_width]

time: 426 us -> 321 us (0.75)
  waiting for transfers between devices: 373 us -> 247 us
  starting transfers between devices: 2.79 us -> 22.4 us
    all_gather x1 -> x0, waiting for transfers between devices: 146 us -> none  [per_device(): kv_all = lax.all_gather(kv_pack, CTX, axis=0, tiled=True)]
    all_gather x1, waiting for transfers between devices: 157 us -> 191 us  [per_device(): x_half = lax.all_gather(x_normed, ('xh', 'zz'), axis=0, tiled=True)]
    all_gather x1, waiting for transfers between devices: 22.5 us -> 0.63 us  [per_device(): pair_weights = lax.all_gather(both_weights, 'cc', axis=1, tiled=True)]
    all_to_all x0 -> x1, starting transfers between devices: none -> 19.6 us  [per_device(): lax.all_to_all(jnp.stack([kv_pack] * lax.axis_size(CTX)), CTX, 0, 0)]
    reduce_scatter x1, waiting for transfers between devices: 47.3 us -> 55.2 us  [per_device(): lax.psum_scatter(block_terms, 'mp', scatter_dimension=0, tiled=True)]
  transfers between devices with their start and end apart: 5 -> 5, of which waited for: 4 -> 3; matrix products, arithmetic and copies ran while one was open for 6% -> 9% of each run, Pallas kernels for 0% -> 0%
where the time goes in v1:
time: 321 us; the launch traced here: 320 us
  waiting for transfers between devices  247 us (77%)
  starting transfers between devices  22.4 us (7%)
  matrix products  15.9 us (5%)
  between operations  13.9 us (4%)
  other arithmetic  11 us (3%)
  local copies, waits for them, and re-layouts  9.54 us (3%)
    all_gather x1, waiting for transfers between devices, per_device(): x_half = lax.all_gather(x_normed, ('xh', 'zz'), axis=0, tiled=True)  191 us
    reduce_scatter x1, waiting for transfers between devices, per_device(): lax.psum_scatter(block_terms, 'mp', scatter_dimension=0, tiled=True)  55.2 us
    all_to_all x1, starting transfers between devices, per_device(): lax.all_to_all(jnp.stack([kv_pack] * lax.axis_size(CTX)), CTX, 0, 0)  19.6 us
    dot_general x1, matrix products, per_device(): jnp.dot(x_half, pair_weights, preferred_element_type=jnp.float32)  9.33 us
  transfers between devices with their start and end apart: 5, of which 3 were waited for; matrix products, arithmetic and copies ran while one was open for 9% of the time, Pallas kernels for 0%

profile of v1, /device:TPU:1, one launch (start us, length us, event | category | flops | bytes accessed | tf_op | source)
XLA Modules:
  0.0 320.1 jit_solution(11882140696827384326)
XLA Ops:
  7.2 0.0 copy-start
  7.2 0.0 all-gather.3.cloned.1.call-start
  7.2 2.3 pad_maximum_fusion
  9.5 0.0 all-gather.3.cloned.1.call-update
  9.5 0.0 all-gather.5.cloned.1.call-start
  9.6 0.7 all-gather.5.cloned.1.call-update
  10.3 0.8 copy.21
  11.1 0.8 copy.20
  12.0 0.7 compare_reduce_fusion.1
  12.6 0.6 compare_reduce_fusion
  13.2 1.3 fusion.32
  14.6 0.7 fusion.31
  15.3 0.1 copy.22
  15.4 2.2 stack.14
  17.6 19.6 %all-to-all-start = ((bf16[64,64,384]{2,1,0:T(8,128)(2,1)}), bf16[64,64,384]{2,1,0:T(8,128)(2,1)S(1)}, u32[]{:S(2)}, u32[]{:S(2)}) async-start(bf16[64,64,384]{2,1,0:T(8,128)(2,1)} %stack.14), calls=%async_computation | async-start | bytes 6291456 | tf_op jit(solution)/shard_map/all_to_all | solution.py:25
  37.2 0.0 reduce-scatter.2.cloned.1.call-start
  37.3 0.6 all-gather.3.cloned.1.call-done
  37.9 190.8 %all-gather.5.cloned.1.call-done = bf16[2048,1024]{1,0:T(8,128)(2,1)} async-done(((bf16[64,1024]{1,0:T(8,128)(2,1)}), bf16[2048,1024]{1,0:T(8,128)(2,1)}) %all-gather.5.cloned.1.call-update) | async-done | bytes 4194320 | tf_op jit(solution)/shard_map/all_gather | solution.py:59
  228.7 9.3 %convert_bitcast_fusion = bf16[2048,1024]{0,1:T(8,128)(2,1)} fusion(bf16[1024,1024]{1,0:T(8,128)(2,1)} %all-gather.3.cloned.1.call-done, bf16[2048,1024]{1,0:T(8,128)(2,1)} %all-gather.5.cloned.1.call-done), kind=kOutput, calls=%fused_computation.8 | convolution fusion | flops 4297064448 | bytes 10485760 | tf_op jit(solution)/shard_map/dot_general | solution.py:60
  238.0 0.0 copy-start.2
  238.0 0.0 reduce-scatter.2.cloned.1.call-update
  238.0 0.6 copy-done.2
  238.7 0.0 all-to-all-done
  238.7 0.1 slice_convert_fusion
  238.8 1.2 fusion.9
  240.0 0.2 broadcast_compare_fusion
  240.2 0.0 copy-done
  240.2 1.7 fusion
  241.9 0.0 copy-start.1
  241.9 3.2 %copy-done.1 = f32[4096,64,8]{0,1,2:T(8,128)} copy-done((f32[4096,64,8]{0,1,2:T(8,128)}, f32[4096,64,8]{0,1,2:T(8,128)S(1)}, u32[]{:S(2)}) %copy-start.1) | copy-done | bytes 8388632
  245.1 2.4 fusion.3
  247.6 55.2 %reduce-scatter.2.cloned.1.call-done = bf16[256,1024]{0,1:T(8,128)(2,1)} async-done(((bf16[2048,1024]{0,1:T(8,128)(2,1)}), bf16[256,1024]{0,1:T(8,128)(2,1)}) %reduce-scatter.2.cloned.1.call-update) | async-done | bytes 524304 | tf_op jit(solution)/shard_map/reduce_scatter | solution.py:63
  302.8 1.1 convert_element_type.53
  303.9 0.2 fusion.30
  304.1 0.1 fusion.25
  304.2 2.6 collective-permute-start
  306.8 4.9 %fusion.16 = bf16[64,1,8,128]{3,0,2,1:T(8,128)(2,1)S(1)} fusion(f32[4096,64,8]{0,1,2:T(8,128)} %copy-done.1, f32[8,64]{1,0:T(8,128)S(1)} %broadcast_maximum_fusion, pred[64,4096]{1,0:T(8,128)(4,1)S(1)} %broadcast_compare_fusion, bf16[4096,384]{1,0:T(8,128)(2,1)S(1)} %bitcast.81, f32[8,64]{1,0:T(8,128)S(1)} %fusion.3), kind=kOutput, calls=%fused_computation.16 | convolution fusion | flops 545390592 | bytes 9838592 | tf_op jit(solution)/shard_map/gjts,sgd->gjtd/dot_general | solution.py:45
  311.8 0.1 copy.24
  311.9 0.7 copy.37
  312.5 0.0 collective-permute-done
  312.5 0.1 fusion.23
  312.6 0.1 copy.26
  312.8 0.1 copy.25
  312.9 0.7 copy.27
  (6 shorter events, 0.1 us)
Async XLA Ops:
  7.2 233.0 %copy-start = (bf16[64,1024]{1,0:T(8,128)(2,1)S(1)}, bf16[64,1024]{1,0:T(8,128)(2,1)}, u32[]{:S(2)}) copy-start(bf16[64,1024]{1,0:T(8,128)(2,1)} %param.11) | copy-start | bytes 393220
  7.2 30.7 %all-gather.3.cloned.1.call-start = ((), (), s32[]{:S(2)}) async-start(), calls=%async_computation.2 | async-start | bytes 3145728 | tf_op jit(solution)/shard_map/all_gather | solution.py:58
  9.5 219.1 %all-gather.5.cloned.1.call-start = ((), (), s32[]{:S(2)}) async-start(), calls=%async_computation.3 | async-start | bytes 4325376 | tf_op jit(solution)/shard_map/all_gather | solution.py:59
  17.6 221.1 %all-to-all-start = ((bf16[64,64,384]{2,1,0:T(8,128)(2,1)}), bf16[64,64,384]{2,1,0:T(8,128)(2,1)S(1)}, u32[]{:S(2)}, u32[]{:S(2)}) async-start(bf16[64,64,384]{2,1,0:T(8,128)(2,1)} %stack.14), calls=%async_computation | async-start | bytes 6291456 | tf_op jit(solution)/shard_map/all_to_all | solution.py:25
  37.2 265.6 %reduce-scatter.2.cloned.1.call-start = ((), (), s32[]{:S(2)}) async-start(), calls=%async_computation.4 | async-start | bytes 4718592 | tf_op jit(solution)/shard_map/reduce_scatter | solution.py:63
  238.0 0.7 copy-start.2
  241.9 3.2 %copy-start.1 = (f32[4096,64,8]{0,1,2:T(8,128)}, f32[4096,64,8]{0,1,2:T(8,128)S(1)}, u32[]{:S(2)}) copy-start(f32[4096,64,8]{0,1,2:T(8,128)S(1)} %get-tuple-element.35) | copy-start | bytes 25165828
  304.2 8.4 %collective-permute-start = (bf16[256,256]{0,1:T(8,128)(2,1)S(1)}, bf16[256,256]{0,1:T(8,128)(2,1)S(1)}, u32[]{:S(2)}, u32[]{:S(2)}) collective-permute-start(bf16[256,256]{0,1:T(8,128)(2,1)S(1)} %get-tuple-element.32), channel_id=1, source_target_pairs={{0,8},{8,0},{1,9},{9,1},{2,10},{10,2},{3,11},{11,3},{4,12},{12,4},... | collective-permute-start | bytes 393224 | tf_op jit(solution)/shard_map/ppermute | solution.py:76
Sparse Core Ops, SparseCore 0:
  10.1 27.7 all-gather.2
  41.0 187.6 all-gather.4
  238.2 64.5 reduce-scatter.1
